TPU v7x, 256 devices: a whole 4x4x8 slice. The times are simulated.
256 devices in a mesh: grp: 8 (over x_hi, y), dev: 32 (over z, x_lo, core).
Axes of the slice: x: 4 (x_hi: 2, x_lo: 2; x = x_hi * 2 + x_lo), y: 4, z: 8, core: 2. Of those that a mesh axis runs over, the one named last changes fastest.
Arguments:
- slab: bfloat16 [16, 8000, 8000], P('grp', 'dev'), may hold values from -2.5 to 2.5
- orbitals: bfloat16 [8000, 640], P('dev'), may hold values from -0.0625 to 0.0625
- hcore: float32 [8000, 8000], P('dev', 'grp'), may hold values from -6 to 6
- metric_inv: float32 [16, 16], replicated, may hold values from -1 to 2, as said below
Outputs:
- fock: float32 [8000, 8000], P('dev', 'grp')
Inputs may be any that keep to these rules, and one draw needn't show every extreme that they name: `metric_inv`: symmetric.
All inputs are finite; a program needn't handle non-finite values.
Results may differ from a plain program's by a relative error of at most 0.0065.
Values may be sent and summed in bfloat16 or wider, within the bound.
No kernel may reach another device: no remote copies, remote signals or barrier semaphores. Data moves between devices by JAX's collectives and lax.ppermute only.
A program may use at most 192 MiB of HBM per device.

v0:
```python
import jax
import jax.numpy as jnp
from jax import lax
from jax.sharding import PartitionSpec as P


def shards(slab, orbitals, hcore, metric_inv):
    aux_count = slab.shape[0]
    row_count = slab.shape[1]
    full_width = slab.shape[2]
    occ_count = orbitals.shape[1]
    slab_flat = slab.reshape(aux_count * row_count, full_width)
    half_done = jnp.dot(
        slab_flat,
        lax.all_gather(orbitals, "dev", axis=0, tiled=True),
        preferred_element_type=jnp.float32,
    )
    half_done = half_done.astype(jnp.bfloat16).reshape(aux_count, row_count, occ_count)
    aux_density = jnp.sum(
        half_done.astype(jnp.float32) * orbitals.astype(jnp.float32)[None], axis=(1, 2)
    )
    group_index = lax.axis_index("grp")
    group_density = lax.psum(aux_density, "dev")
    density_all = lax.all_gather(group_density, "grp", axis=0, tiled=True)
    fit_coef = jnp.dot(metric_inv, density_all, precision=lax.Precision.HIGHEST)
    half_flat = jnp.transpose(half_done, (1, 0, 2)).reshape(row_count, aux_count * occ_count)
    exchange_part = lax.dot_general(
        half_flat,
        lax.all_gather(half_flat, "dev", axis=0, tiled=True),
        (((1,), (1,)), ((), ())),
        preferred_element_type=jnp.float32,
    )
    local_coef = lax.dynamic_slice_in_dim(fit_coef, group_index * aux_count, aux_count)
    coulomb_part = jnp.zeros((row_count, full_width), jnp.float32)
    for aux_index in range(aux_count):
        coulomb_part = coulomb_part + local_coef[aux_index] * slab[aux_index].astype(jnp.float32)
    reduced = lax.psum_scatter(
        2.0 * coulomb_part - exchange_part, "grp", scatter_dimension=1, tiled=True
    )
    fock = hcore + reduced
    return fock


def solution(mesh):
    return jax.shard_map(
        shards,
        mesh=mesh,
        in_specs=(P("grp", "dev", None), P("dev", None), P("dev", "grp"), P()),
        out_specs=P("dev", "grp"),
        check_vma=False,
    )
```

profile of v0, /device:TPU:1, one launch (start us, length us, event | category | flops | bytes accessed | tf_op | source)
XLA Modules:
  0.0 403.7 jit_solution(6335460769524792547)
XLA Ops:
  6.5 0.0 copy-start
  6.5 0.0 all-gather.5.cloned.1.call-start
  6.5 0.7 all-gather.5.cloned.1.call-update
  7.3 0.0 all-gather.7.cloned.1.call-start
  7.3 1.1 mul.37
  8.4 0.1 mul.38
  8.5 7.4 %copy.19 = bf16[2,250,8000]{2,1,0:T(8,128)(2,1)} copy(bf16[2,250,8000]{2,0,1:T(2,128)(2,1)} %param.4) | data formatting | bytes 16000000 | tf_op args[0]
  15.9 10.1 %reshape.21 = bf16[500,8000]{1,0:T(8,128)(2,1)} reshape(bf16[2,250,8000]{2,1,0:T(8,128)(2,1)} %copy.19) | data formatting | bytes 16000000 | tf_op jit(solution)/shard_map/reshape | solution.py:12
  25.9 61.7 %all-gather.5.cloned.1.call-done = bf16[32,250,640]{2,1,0:T(8,128)(2,1)} async-done(((bf16[1,250,640]{2,1,0:T(8,128)(2,1)}), bf16[32,250,640]{2,1,0:T(8,128)(2,1)}) %all-gather.5.cloned.1.call-update) | async-done | bytes 10240016 | tf_op jit(solution)/shard_map/all_gather | solution.py:15
  87.6 10.9 %reshape.28 = bf16[8000,640]{1,0:T(8,128)(2,1)} reshape(bf16[32,250,640]{2,1,0:T(8,128)(2,1)} %all-gather.5.cloned.1.call-done) | data formatting | bytes 20480000
  98.5 12.2 %multiply_reduce_fusion = (f32[500]{0:T(512)S(1)}, bf16[500,640]{1,0:T(8,128)(2,1)S(1)}) fusion(f32[500,640]{1,0:T(8,128)S(1)} %mul.38, bf16[500,8000]{1,0:T(8,128)(2,1)} %reshape.21, bf16[8000,640]{1,0:T(8,128)(2,1)} %reshape.28), kind=kOutput, calls=%fused_computation.2 | convolution fusion | flops 5121279488 | bytes 20162000 | tf_op jit(solution)/shard_map/dot_general | solution.py:13
  110.8 0.1 reshape.22
  110.9 0.3 copy.22
  111.2 1.1 copy.24
  112.2 0.0 all-gather.7.cloned.1.call-update
  112.3 0.0 reduce-scatter.2.cloned.1.call-start
  112.3 17.1 %fusion.1 = (bf16[1,250,8000]{2,0,1:T(2,128)(2,1)}, bf16[1,250,8000]{2,0,1:T(2,128)(2,1)}) fusion(bf16[2,250,8000]{2,0,1:T(2,128)(2,1)} %param.4), kind=kLoop, calls=%fused_computation.5 | loop fusion | bytes 16000000 | tf_op jit(solution)/shard_map/slice | solution.py:36
  129.5 17.3 %copy.25 = bf16[1,250,8000]{1,2,0:T(8,128)(2,1)} copy(bf16[1,250,8000]{2,0,1:T(2,128)(2,1)} %get-tuple-element.5) | data formatting | bytes 8000000
  146.8 0.0 copy-start.2
  146.8 17.4 %copy.26 = bf16[1,250,8000]{1,2,0:T(8,128)(2,1)} copy(bf16[1,250,8000]{2,0,1:T(2,128)(2,1)} %get-tuple-element.6) | data formatting | bytes 8000000
  164.1 0.0 copy-done.2
  164.1 0.6 dynamic-slice.1
  164.7 0.1 reduce_sum.14
  164.8 0.1 reduce_sum.18
  165.5 54.1 %psum.7 = f32[2]{0:T(128)S(1)} all-reduce(f32[2]{0:T(128)S(1)} %reduce_sum.18), channel_id=1, replica_groups=mesh['grp'=8,'dev'=32] {'dev'}, use_global_device_ids=true, to_apply=%region_2.0 | all-reduce | flops 2 | bytes 16 | tf_op jit(solution)/shard_map/psum | solution.py:23
  219.7 0.2 dynamic-update-slice
  219.9 20.7 %all-reduce = f32[16]{0:T(128)S(1)} all-reduce(f32[16]{0:T(128)S(1)} %dynamic-update-slice), channel_id=1, replica_groups=mesh['grp'=8,'dev'=32] {'grp'}, use_global_device_ids=true, to_apply=%add | all-reduce | flops 16 | bytes 128
  240.6 0.0 copy-done
  240.6 0.1 convolution_bitcast_fusion
  240.7 0.1 dynamic_slice.3
  240.8 0.6 fusion.2
  241.4 0.0 all-gather.7.cloned.1.call-done
  241.4 17.5 %reshape.30 = bf16[8000,1280]{1,0:T(8,128)(2,1)} reshape(bf16[32,250,1280]{2,1,0:T(8,128)(2,1)} %all-gather.7.cloned.1.call-done) | data formatting | bytes 40960000
  258.9 15.5 %convolution_subtract_fusion = f32[250,8000]{0,1:T(8,128)} fusion(bf16[250,1280]{0,1:T(8,128)(2,1)S(1)} %bitcast.20, bf16[8000,1280]{1,0:T(8,128)(2,1)} %reshape.30, bf16[1,250,8000]{1,2,0:T(8,128)(2,1)} %copy.26, bf16[1,250,8000]{1,2,0:T(8,128)(2,1)} %copy.25, f32[]{:T(128)} %bitcast.5, f32[]{:T(128)} %bitcast.4), kind=kOutput, calls=%fused_computation | convolution fusion | flops 5134000128 | bytes 37120008 | tf_op jit(solution)/shard_map/dot_general | solution.py:27
  274.4 0.0 copy-start.1
  274.4 0.0 reduce-scatter.2.cloned.1.call-update
  274.4 120.3 %reduce-scatter.2.cloned.1.call-done = f32[250,1000]{0,1:T(8,128)} async-done(((f32[250,8000]{0,1:T(8,128)}), f32[250,1000]{0,1:T(8,128)}) %reduce-scatter.2.cloned.1.call-update) | async-done | bytes 1000016 | tf_op jit(solution)/shard_map/reduce_scatter | solution.py:37
  394.8 0.0 copy-done.1
  394.8 2.4 add.16
  (1 shorter events, 0.0 us)
Async XLA Ops:
  6.5 234.0 %copy-start = (f32[16,16]{1,0:T(8,128)S(1)}, f32[16,16]{1,0:T(8,128)}, u32[]{:S(2)}) copy-start(f32[16,16]{1,0:T(8,128)} %param.7) | copy-start | bytes 3076
  6.5 81.1 %all-gather.5.cloned.1.call-start = ((), (), s32[]{:S(2)}) async-start(), calls=%async_computation.2 | async-start | bytes 10813440 | tf_op jit(solution)/shard_map/all_gather | solution.py:15
  7.3 234.1 %all-gather.7.cloned.1.call-start = ((), (), s32[]{:S(2)}) async-start(), calls=%async_computation.3 | async-start | bytes 21626880 | tf_op jit(solution)/shard_map/all_gather | solution.py:29
  112.3 282.5 %reduce-scatter.2.cloned.1.call-start = ((), (), s32[]{:S(2)}) async-start(), calls=%async_computation.1 | async-start | bytes 9216000 | tf_op jit(solution)/shard_map/reduce_scatter | solution.py:37
  146.8 17.4 %copy-start.2 = (u32[256]{0:T(256)S(1)}, u32[256]{0:T(256)}, u32[]{:S(2)}) copy-start(u32[256]{0:T(256)} %constant.21) | copy-start | bytes 3076
  274.4 120.4 %copy-start.1 = (f32[250,1000]{0,1:T(8,128)S(1)}, f32[250,1000]{0,1:T(8,128)}, u32[]{:S(2)}) copy-start(f32[250,1000]{0,1:T(8,128)} %param.6) | copy-start | bytes 3000004
Sparse Core Ops, SparseCore 0:
  9.2 78.3 all-gather.4
  112.4 121.4 all-gather.6
  274.5 120.1 reduce-scatter.1
where the time goes:
time: 405 us; the launch traced here: 404 us
  waiting for transfers between devices  183 us (45%)
  local copies, waits for them, and re-layouts  102 us (25%)
  blocking collectives  74.8 us (18%)
  matrix products  27.8 us (7%)
  between operations  13.8 us (3%)
    reduce_scatter x1, waiting for transfers between devices, shards(): lax.psum_scatter(2.0 * coulomb_part - exchange_part, 'grp', scatter_dimen...  120 us
    unnamed x15, local copies, waits for them, and re-layouts  72.4 us
    all_gather x1, waiting for transfers between devices, shards(): lax.all_gather(orbitals, 'dev', axis=0, tiled=True)  61.7 us
    psum x1, blocking collectives, shards(): group_density = lax.psum(aux_density, 'dev')  54.1 us
    unnamed x1, blocking collectives  20.7 us
    slice x1, local copies, waits for them, and re-layouts, shards(): slab[aux_index].astype(jnp.float32)  17.1 us
    dot_general x1, matrix products, shards(): lax.dot_general(half_flat, lax.all_gather(half_flat, 'dev', axis=0, tiled...  15.5 us
    dot_general x1, matrix products, shards(): jnp.dot(slab_flat, lax.all_gather(orbitals, 'dev', axis=0, tiled=True), p...  12.2 us
  transfers between devices with their start and end apart: 3, of which 2 were waited for; matrix products, arithmetic and copies ran while one was open for 18% of the time, Pallas kernels for 0%

commit v1 on v0

--- a/solution.py
+++ b/solution.py
@@ -12,7 +12,9 @@
     slab_flat = slab.reshape(aux_count * row_count, full_width)
     half_done = jnp.dot(
         slab_flat,
-        lax.all_gather(orbitals, "dev", axis=0, tiled=True),
+        jnp.concatenate(
+            lax.all_to_all(jnp.stack([orbitals] * lax.axis_size("dev")), "dev", 0, 0), axis=0
+        ),
         preferred_element_type=jnp.float32,
     )
     half_done = half_done.astype(jnp.bfloat16).reshape(aux_count, row_count, occ_count)

time: 405 us -> 572 us (1.41)
  waiting for transfers between devices: 183 us -> 332 us
  starting transfers between devices: 0.08 us -> 11.3 us
    all_to_all x0 -> x1, waiting for transfers between devices: none -> 214 us  [shards(): lax.all_to_all(jnp.stack([orbitals] * lax.axis_size('dev')), 'dev', 0, 0)]
    all_gather x1 -> x0, waiting for transfers between devices: 61.7 us -> none  [shards(): lax.all_gather(orbitals, 'dev', axis=0, tiled=True)]
    all_to_all x0 -> x1, starting transfers between devices: none -> 11.2 us  [shards(): lax.all_to_all(jnp.stack([orbitals] * lax.axis_size('dev')), 'dev', 0, 0)]
    unnamed x15 -> x16, local copies, waits for them, and re-layouts: 72.4 us -> 61.3 us
    reshape x0 -> x1, local copies, waits for them, and re-layouts: none -> 10.9 us  [shards(): jnp.concatenate(lax.all_to_all(jnp.stack([orbitals] * lax.axis_size('dev'...]
    another operation x0 -> x1, local copies, waits for them, and re-layouts: none -> 6.23 us  [shards(): jnp.stack([orbitals] * lax.axis_size('dev'))]
  transfers between devices with their start and end apart: 3 -> 3, of which waited for: 2 -> 2; matrix products, arithmetic and copies ran while one was open for 18% -> 12% of each run, Pallas kernels for 0% -> 0%
where the time goes in v1:
time: 572 us; the launch traced here: 570 us
  waiting for transfers between devices  332 us (58%)
  local copies, waits for them, and re-layouts  107 us (19%)
  blocking collectives  75.1 us (13%)
  matrix products  27.8 us (5%)
  between operations  14.1 us (2%)
  starting transfers between devices  11.3 us (2%)
    all_to_all x1, waiting for transfers between devices, shards(): lax.all_to_all(jnp.stack([orbitals] * lax.axis_size('dev')), 'dev', 0, 0)  214 us
    reduce_scatter x1, waiting for transfers between devices, shards(): lax.psum_scatter(2.0 * coulomb_part - exchange_part, 'grp', scatter_dimen...  119 us
    unnamed x16, local copies, waits for them, and re-layouts  61.3 us
    psum x1, blocking collectives, shards(): group_density = lax.psum(aux_density, 'dev')  54.6 us
    unnamed x1, blocking collectives  20.5 us
    slice x1, local copies, waits for them, and re-layouts, shards(): slab[aux_index].astype(jnp.float32)  17.1 us
    dot_general x1, matrix products, shards(): lax.dot_general(half_flat, lax.all_gather(half_flat, 'dev', axis=0, tiled...  15.5 us
    dot_general x1, matrix products, shards(): jnp.dot(slab_flat, jnp.concatenate(lax.all_to_all(jnp.stack([orbitals] *...  12.2 us
  transfers between devices with their start and end apart: 3, of which 2 were waited for; matrix products, arithmetic and copies ran while one was open for 12% of the time, Pallas kernels for 0%

profile of v1, /device:TPU:1, one launch (start us, length us, event | category | flops | bytes accessed | tf_op | source)
XLA Modules:
  0.0 570.2 jit_solution(920191631142687440)
XLA Ops:
  6.5 0.0 copy-start
  6.5 6.2 %stack.2 = bf16[32,250,640]{2,1,0:T(8,128)(2,1)} broadcast(bf16[250,640]{1,0:T(8,128)(2,1)} %param.5), dimensions={1,2} | broadcast | bytes 10560000 | tf_op jit(solution)/shard_map/stack | solution.py:16
  12.8 0.0 copy-start.1
  12.8 11.2 %all-to-all-start = ((bf16[32,250,640]{2,1,0:T(8,128)(2,1)}), bf16[32,250,640]{2,1,0:T(8,128)(2,1)}, u32[]{:S(2)}, u32[]{:S(2)}) async-start(bf16[32,250,640]{2,1,0:T(8,128)(2,1)} %stack.2), calls=%async_computation | async-start | bytes 20971520 | tf_op jit(solution)/shard_map/all_to_all | solution.py:16
  24.0 0.0 all-gather.3.cloned.1.call-start
  24.1 0.0 copy-done.1
  24.1 0.1 mul.37
  24.2 0.1 mul.38
  24.3 7.3 %copy.19 = bf16[2,250,8000]{2,1,0:T(8,128)(2,1)} copy(bf16[2,250,8000]{2,0,1:T(2,128)(2,1)} %param.4) | data formatting | bytes 16000000 | tf_op args[0]
  31.6 10.0 %reshape.26 = bf16[500,8000]{1,0:T(8,128)(2,1)} reshape(bf16[2,250,8000]{2,1,0:T(8,128)(2,1)} %copy.19) | data formatting | bytes 16000000 | tf_op jit(solution)/shard_map/reshape | solution.py:12
  41.6 213.8 %all-to-all-done = bf16[32,250,640]{2,1,0:T(8,128)(2,1)} async-done(((bf16[32,250,640]{2,1,0:T(8,128)(2,1)}), bf16[32,250,640]{2,1,0:T(8,128)(2,1)}, u32[]{:S(2)}, u32[]{:S(2)}) %all-to-all-start) | async-done | bytes 10240032 | tf_op jit(solution)/shard_map/all_to_all | solution.py:16
  255.4 10.9 %reshape.27 = bf16[8000,640]{1,0:T(8,128)(2,1)} reshape(bf16[32,250,640]{2,1,0:T(8,128)(2,1)} %all-to-all-done) | data formatting | bytes 20480000 | tf_op jit(solution)/shard_map/reshape | solution.py:15
  266.4 12.2 %multiply_reduce_fusion = (f32[500]{0:T(512)S(1)}, bf16[500,640]{1,0:T(8,128)(2,1)S(1)}) fusion(f32[500,640]{1,0:T(8,128)S(1)} %mul.38, bf16[500,8000]{1,0:T(8,128)(2,1)} %reshape.26, bf16[8000,640]{1,0:T(8,128)(2,1)} %reshape.27), kind=kOutput, calls=%fused_computation.2 | convolution fusion | flops 5121279488 | bytes 20162000 | tf_op jit(solution)/shard_map/dot_general | solution.py:13
  278.6 0.1 reshape.28
  278.7 0.3 copy.22
  279.0 1.1 copy.24
  280.1 0.0 all-gather.3.cloned.1.call-update
  280.1 0.0 reduce-scatter.2.cloned.1.call-start
  280.1 17.1 %fusion.1 = (bf16[1,250,8000]{2,0,1:T(2,128)(2,1)}, bf16[1,250,8000]{2,0,1:T(2,128)(2,1)}) fusion(bf16[2,250,8000]{2,0,1:T(2,128)(2,1)} %param.4), kind=kLoop, calls=%fused_computation.5 | loop fusion | bytes 16000000 | tf_op jit(solution)/shard_map/slice | solution.py:38
  297.3 17.3 %copy.25 = bf16[1,250,8000]{1,2,0:T(8,128)(2,1)} copy(bf16[1,250,8000]{2,0,1:T(2,128)(2,1)} %get-tuple-element.5) | data formatting | bytes 8000000
  314.6 0.0 copy-start.3
  314.6 17.3 %copy.26 = bf16[1,250,8000]{1,2,0:T(8,128)(2,1)} copy(bf16[1,250,8000]{2,0,1:T(2,128)(2,1)} %get-tuple-element.6) | data formatting | bytes 8000000
  331.9 0.0 copy-done.3
  331.9 0.6 dynamic-slice.1
  332.5 0.1 reduce_sum.14
  332.6 0.1 reduce_sum.18
  333.3 54.6 %psum.7 = f32[2]{0:T(128)S(1)} all-reduce(f32[2]{0:T(128)S(1)} %reduce_sum.18), channel_id=1, replica_groups=mesh['grp'=8,'dev'=32] {'dev'}, use_global_device_ids=true, to_apply=%region_2.0 | all-reduce | flops 2 | bytes 16 | tf_op jit(solution)/shard_map/psum | solution.py:25
  387.9 0.2 dynamic-update-slice
  388.1 20.5 %all-reduce = f32[16]{0:T(128)S(1)} all-reduce(f32[16]{0:T(128)S(1)} %dynamic-update-slice), channel_id=1, replica_groups=mesh['grp'=8,'dev'=32] {'grp'}, use_global_device_ids=true, to_apply=%add | all-reduce | flops 16 | bytes 128
  408.6 0.0 copy-done
  408.6 0.1 convolution_bitcast_fusion
  408.7 0.1 dynamic_slice.3
  408.8 0.6 fusion.2
  409.4 0.0 all-gather.3.cloned.1.call-done
  409.4 17.5 %reshape.34 = bf16[8000,1280]{1,0:T(8,128)(2,1)} reshape(bf16[32,250,1280]{2,1,0:T(8,128)(2,1)} %all-gather.3.cloned.1.call-done) | data formatting | bytes 40960000
  426.9 15.5 %convolution_subtract_fusion = f32[250,8000]{0,1:T(8,128)} fusion(bf16[250,1280]{0,1:T(8,128)(2,1)S(1)} %bitcast.19, bf16[8000,1280]{1,0:T(8,128)(2,1)} %reshape.34, bf16[1,250,8000]{1,2,0:T(8,128)(2,1)} %copy.26, bf16[1,250,8000]{1,2,0:T(8,128)(2,1)} %copy.25, f32[]{:T(128)} %bitcast.4, f32[]{:T(128)} %bitcast.3), kind=kOutput, calls=%fused_computation | convolution fusion | flops 5134000128 | bytes 37120008 | tf_op jit(solution)/shard_map/dot_general | solution.py:29
  442.4 0.0 copy-start.2
  442.4 0.0 reduce-scatter.2.cloned.1.call-update
  442.4 118.6 %reduce-scatter.2.cloned.1.call-done = f32[250,1000]{0,1:T(8,128)} async-done(((f32[250,8000]{0,1:T(8,128)}), f32[250,1000]{0,1:T(8,128)}) %reduce-scatter.2.cloned.1.call-update) | async-done | bytes 1000016 | tf_op jit(solution)/shard_map/reduce_scatter | solution.py:39
  561.0 0.0 copy-done.2
  561.0 2.4 add.16
  (1 shorter events, 0.0 us)
Async XLA Ops:
  6.5 402.1 %copy-start = (f32[16,16]{1,0:T(8,128)S(1)}, f32[16,16]{1,0:T(8,128)}, u32[]{:S(2)}) copy-start(f32[16,16]{1,0:T(8,128)} %param.7) | copy-start | bytes 3076
  12.8 11.3 %copy-start.1 = (bf16[250,640]{1,0:T(8,128)(2,1)S(1)}, bf16[250,640]{1,0:T(8,128)(2,1)}, u32[]{:S(2)}) copy-start(bf16[250,640]{1,0:T(8,128)(2,1)} %param.5) | copy-start | bytes 960004
  12.8 242.7 %all-to-all-start = ((bf16[32,250,640]{2,1,0:T(8,128)(2,1)}), bf16[32,250,640]{2,1,0:T(8,128)(2,1)}, u32[]{:S(2)}, u32[]{:S(2)}) async-start(bf16[32,250,640]{2,1,0:T(8,128)(2,1)} %stack.2), calls=%async_computation | async-start | bytes 20971520 | tf_op jit(solution)/shard_map/all_to_all | solution.py:16
  24.0 385.4 %all-gather.3.cloned.1.call-start = ((), (), s32[]{:S(2)}) async-start(), calls=%async_computation.3 | async-start | bytes 21626880 | tf_op jit(solution)/shard_map/all_gather | solution.py:31
  280.1 280.9 %reduce-scatter.2.cloned.1.call-start = ((), (), s32[]{:S(2)}) async-start(), calls=%async_computation.2 | async-start | bytes 9216000 | tf_op jit(solution)/shard_map/reduce_scatter | solution.py:39
  314.6 17.3 %copy-start.3 = (u32[256]{0:T(256)S(1)}, u32[256]{0:T(256)}, u32[]{:S(2)}) copy-start(u32[256]{0:T(256)} %constant.21) | copy-start | bytes 3076
  442.4 118.6 %copy-start.2 = (f32[250,1000]{0,1:T(8,128)S(1)}, f32[250,1000]{0,1:T(8,128)}, u32[]{:S(2)}) copy-start(f32[250,1000]{0,1:T(8,128)} %param.6) | copy-start | bytes 3000004
Sparse Core Ops, SparseCore 0:
  280.2 119.0 all-gather.2
  442.6 118.3 reduce-scatter.1
